TPU v7x, 32 devices: a whole 2x2x4 slice. The times are simulated.
32 devices in a mesh: dp: 4 (over x, core), seq: 2 (over y), head: 4 (over z).
Axes of the slice: x: 2, y: 2, z: 4, core: 2. Of those that a mesh axis runs over, the one named last changes fastest.
Arguments:
- embed: bfloat16 [4, 1024, 1536], P('dp', 'seq', 'head'), may hold values from -6 to 6
- donor_pos: int32 [4, 256], P('dp', 'seq'), may hold values from -1 to 1023, as said below
- acceptor_pos: int32 [4, 256], P('dp', 'seq'), may hold values from -1 to 1023, as said below
- target: bfloat16 [4, 256, 256], P('dp', 'seq'), may hold values from 0 to 4
- donor_w: bfloat16 [1536, 384], P('head'), may hold values from -0.15625 to 0.15625
- acceptor_w: bfloat16 [1536, 384], P('head'), may hold values from -0.15625 to 0.15625
Outputs:
- grad_embed: bfloat16 [4, 1024, 1536], P('dp', 'seq', 'head')
- grad_donor_w: float32 [1536, 384], P('head', 'seq')
- grad_acceptor_w: float32 [1536, 384], P('head', 'seq')
Inputs may be any that keep to these rules, and one draw needn't show every extreme that they name: `donor_pos`: slots k * 128 to (k + 1) * 128 - 1 belong to slab k: they hold one or more positions of k * 512 to (k + 1) * 512 - 1 first, then -1 in the remaining slots. Positions may repeat. `acceptor_pos`: as for donor_pos, drawn independently.
All inputs are finite; a program needn't handle non-finite values.
Results may differ from a plain program's by a relative error of at most 0.02.
Values may be sent and summed in bfloat16 or wider, within the bound.
No kernel may reach another device: no remote copies, remote signals or barrier semaphores. Data moves between devices by JAX's collectives and lax.ppermute only.
A program may use at most 64 MiB of HBM per device.

v0:
```python
import math
import jax
import jax.numpy as jnp
from jax import lax
from jax.sharding import PartitionSpec as P


def site_match(positions, slab_rows, slab_index):
    local_pos = positions - slab_index * slab_rows
    return local_pos[:, :, None] == jnp.arange(slab_rows, dtype=jnp.int32)[None, None, :]


def pair_slope(scores, target, allowed):
    rate = jax.nn.softplus(scores) + 1.0
    return jnp.where(
        allowed, (1.0 - target.astype(jnp.float32) / rate) * jax.nn.sigmoid(scores), 0.0
    ).astype(jnp.bfloat16)


def place_rows(match_bf, values):
    upper = values.astype(jnp.bfloat16)
    lower = (values - upper.astype(jnp.float32)).astype(jnp.bfloat16)
    placed = jnp.einsum("bnr,bnc->brc", match_bf, upper, preferred_element_type=jnp.float32)
    return placed + jnp.einsum("bnr,bnc->brc", match_bf, lower, preferred_element_type=jnp.float32)


def shards(embed, donor_pos, acceptor_pos, target, donor_w, acceptor_w):
    batch, slab_rows, _ = embed.shape
    slab_sites = donor_pos.shape[1]
    width = donor_w.shape[1]
    scale = 1.0 / math.sqrt(width)
    n_seq = lax.axis_size("seq")
    n_head = lax.axis_size("head")
    slab = lax.axis_index("seq")
    sites = slab_sites * n_seq
    target_all = lax.all_gather(target, "seq", axis=1, tiled=True)
    donor_match = site_match(donor_pos, slab_rows, slab).astype(jnp.bfloat16)
    acceptor_match = site_match(acceptor_pos, slab_rows, slab).astype(jnp.bfloat16)
    donor_rows = jnp.einsum(
        "bnr,brc->bnc", donor_match, embed, preferred_element_type=jnp.float32
    ).astype(jnp.bfloat16)
    acceptor_rows = jnp.einsum(
        "bnr,brc->bnc", acceptor_match, embed, preferred_element_type=jnp.float32
    ).astype(jnp.bfloat16)
    donor_part = jnp.einsum(
        "bnc,cp->bnp", donor_rows, donor_w, preferred_element_type=jnp.float32
    ).astype(jnp.bfloat16)
    acceptor_part = jnp.einsum(
        "bnc,cp->bnp", acceptor_rows, acceptor_w, preferred_element_type=jnp.float32
    ).astype(jnp.bfloat16)
    assert slab_sites <= width
    flags = jnp.zeros((batch, 8, width), jnp.bfloat16)
    flags = flags.at[:, 0, :slab_sites].set((donor_pos >= 0).astype(jnp.bfloat16))
    flags = flags.at[:, 1, :slab_sites].set((acceptor_pos >= 0).astype(jnp.bfloat16))
    packed = jnp.concatenate([donor_part, acceptor_part, flags], axis=1)
    gathered = lax.all_gather(packed, ("seq", "head"), axis=1, tiled=False)
    gathered = gathered.reshape(batch, n_seq, n_head, 2 * slab_sites + 8, width)
    donor_total = jnp.zeros((batch, n_seq, slab_sites, width), jnp.float32)
    acceptor_total = jnp.zeros((batch, n_seq, slab_sites, width), jnp.float32)
    for h in range(n_head):
        donor_total = donor_total + gathered[:, :, h, :slab_sites].astype(jnp.float32)
        acceptor_total = acceptor_total + gathered[:, :, h, slab_sites : 2 * slab_sites].astype(
            jnp.float32
        )
    donor_feat_all = donor_total.astype(jnp.bfloat16).reshape(batch, sites, width)
    acceptor_feat_all = acceptor_total.astype(jnp.bfloat16).reshape(batch, sites, width)
    donor_ok_all = (gathered[:, :, 0, 2 * slab_sites, :slab_sites] > 0).reshape(batch, sites)
    acceptor_ok_all = (gathered[:, :, 0, 2 * slab_sites + 1, :slab_sites] > 0).reshape(batch, sites)
    site_slab = jnp.arange(sites, dtype=jnp.int32) // slab_sites
    big = jnp.int32(1 << 30)
    acceptor_tiled = jnp.tile(acceptor_pos, (1, n_seq))
    acceptor_eff = jnp.where(
        site_slab[None, :] == slab,
        acceptor_tiled,
        jnp.where((site_slab[None, :] > slab) & acceptor_ok_all, (slab + 1) * slab_rows, -1),
    )
    donor_tiled = jnp.tile(donor_pos, (1, n_seq))
    donor_eff = jnp.where(
        site_slab[None, :] == slab,
        donor_tiled,
        jnp.where(
            site_slab[None, :] > slab, big, jnp.where(donor_ok_all, slab * slab_rows - 1, -1)
        ),
    )
    donor_feat = lax.dynamic_slice_in_dim(donor_feat_all, slab * slab_sites, slab_sites, 1)
    acceptor_feat = lax.dynamic_slice_in_dim(acceptor_feat_all, slab * slab_sites, slab_sites, 1)
    scores_row = (
        jnp.einsum(
            "bip,bjp->bij", donor_feat, acceptor_feat_all, preferred_element_type=jnp.float32
        )
        * scale
    )
    allowed_row = (donor_pos[:, :, None] >= 0) & (acceptor_eff[:, None, :] > donor_pos[:, :, None])
    slope_row = pair_slope(scores_row, target, allowed_row)
    donor_grad = (
        jnp.einsum("bij,bjp->bip", slope_row, acceptor_feat_all, preferred_element_type=jnp.float32)
        * scale
    ).astype(jnp.bfloat16)
    target_col = lax.dynamic_slice_in_dim(target_all, slab * slab_sites, slab_sites, 2)
    scores_col = (
        jnp.einsum(
            "bip,bjp->bij", donor_feat_all, acceptor_feat, preferred_element_type=jnp.float32
        )
        * scale
    )
    allowed_col = (donor_eff[:, :, None] >= 0) & (acceptor_pos[:, None, :] > donor_eff[:, :, None])
    slope_col = pair_slope(scores_col, target_col, allowed_col)
    acceptor_grad = (
        jnp.einsum("bij,bip->bjp", slope_col, donor_feat_all, preferred_element_type=jnp.float32)
        * scale
    ).astype(jnp.bfloat16)
    donor_site = jnp.einsum("bnp,cp->bnc", donor_grad, donor_w, preferred_element_type=jnp.float32)
    acceptor_site = jnp.einsum(
        "bnp,cp->bnc", acceptor_grad, acceptor_w, preferred_element_type=jnp.float32
    )
    row_grad = place_rows(donor_match, donor_site) + place_rows(acceptor_match, acceptor_site)
    local_dw = jnp.einsum("bnc,bnp->cp", donor_rows, donor_grad, preferred_element_type=jnp.float32)
    local_aw = jnp.einsum(
        "bnc,bnp->cp", acceptor_rows, acceptor_grad, preferred_element_type=jnp.float32
    )
    summed = lax.psum(jnp.stack([local_dw, local_aw]).astype(jnp.bfloat16), ("dp", "seq"))
    part = width // n_seq
    mine = lax.dynamic_slice_in_dim(summed, slab * part, part, 2).astype(jnp.float32)
    return (row_grad.astype(jnp.bfloat16), mine[0], mine[1])


def solution(mesh):
    in_specs = (
        P("dp", "seq", "head"),
        P("dp", "seq"),
        P("dp", "seq"),
        P("dp", "seq", None),
        P("head", None),
        P("head", None),
    )
    out_specs = (P("dp", "seq", "head"), P("head", "seq"), P("head", "seq"))
    return jax.shard_map(shards, mesh=mesh, in_specs=in_specs, out_specs=out_specs, check_vma=False)
```

profile of v0, /device:TPU:0, one launch (start us, length us, event | category | flops | bytes accessed | tf_op | source)
XLA Modules:
  0.0 129.9 jit_solution(11049242850485408550)
XLA Ops:
  7.2 0.0 copy-start
  7.2 0.0 copy-start.5
  7.2 0.0 copy-start.3
  7.2 0.0 all-gather.3.cloned.1.call-start
  7.3 0.7 compare_bitcast_fusion
  8.0 0.7 subtract_bitcast_fusion
  8.7 0.0 copy-done
  8.7 0.3 convolution_convert_fusion.3
  8.9 0.3 convolution_convert_fusion.5
  9.2 1.2 fusion.8
  10.4 0.0 copy-start.4
  10.4 1.2 fusion.7
  11.6 0.2 scatter.14
  11.8 0.7 pad_maximum_fusion.1
  12.5 0.0 all-gather.3.cloned.1.call-update
  12.5 0.0 all-reduce.3.cloned.1.call-start
  12.5 0.0 copy-done.3
  12.6 5.9 %all_gather.11 = bf16[1,256,256]{2,1,0:T(8,128)(2,1)S(1)} all-gather(bf16[1,128,256]{2,1,0:T(8,128)(2,1)S(1)} %copy-done.3), channel_id=1, replica_groups=mesh['dp'=4,'seq'=2,'head'=4] {'seq'}, dimensions={1}, use_global_device_ids=true | all-gather | bytes 196608 | tf_op jit(solution)/shard_map/all_gather | solution.py:36
  18.4 0.0 copy-done.5
  18.4 41.4 %all-gather.3.cloned.1.call-done = bf16[8,264,384]{2,1,0:T(8,128)(2,1)} async-done(((bf16[1,264,384]{2,1,0:T(8,128)(2,1)}), bf16[8,264,384]{2,1,0:T(8,128)(2,1)}) %all-gather.3.cloned.1.call-update) | async-done | bytes 1622032 | tf_op jit(solution)/shard_map/all_gather | solution.py:56
  59.8 0.0 copy-start.1
  59.8 1.7 %add_convert_fusion.1 = (bf16[1,2,1,128,384]{4,3,2,1,0:T(8,128)(2,1)S(1)}, bf16[1,2,1,128,384]{4,3,2,1,0:T(8,128)(2,1)S(1)}) fusion(bf16[1,2,4,264,384]{4,3,2,1,0:T(8,128)(2,1)} %bitcast.139), kind=kLoop, calls=%fused_computation.28 | loop fusion | flops 1572864 | bytes 1966080 | tf_op jit(solution)/shard_map/convert.9
  61.5 0.8 fusion.91
  62.3 0.0 copy-done.4
  62.3 0.6 fusion.6
  62.8 0.0 copy-done.1
  62.8 0.0 copy-start.2
  62.9 0.2 fusion.93
  63.1 0.3 fusion.4
  63.4 0.5 fusion.5
  63.9 0.0 copy-done.2
  63.9 0.2 fusion.92
  64.2 0.3 fusion.3
  64.4 0.4 fusion.12
  64.8 0.4 convolution_add_fusion.1
  65.2 0.9 pad_maximum_fusion
  66.1 0.0 all-reduce.3.cloned.1.call-update
  66.1 0.4 fusion.11
  66.5 1.1 fusion.2
  67.6 52.4 %all-reduce.3.cloned.1.call-done = bf16[2,384,384]{2,1,0:T(8,128)(2,1)} async-done(((bf16[2,384,384]{2,1,0:T(8,128)(2,1)}), bf16[2,384,384]{2,1,0:T(8,128)(2,1)}) %all-reduce.3.cloned.1.call-update) | async-done | bytes 589840 | tf_op jit(solution)/shard_map/psum | solution.py:121
  120.0 1.2 dynamic-slice_convert_fusion
  121.3 0.1 slice_bitcast_fusion
  121.3 0.9 copy.17
  122.2 0.9 copy.18
  (4 shorter events, 0.0 us)
Async XLA Ops:
  7.2 1.5 %copy-start = (bf16[1,512,384]{2,1,0:T(8,128)(2,1)S(1)}, bf16[1,512,384]{2,1,0:T(8,128)(2,1)}, u32[]{:S(2)}) copy-start(bf16[1,512,384]{2,1,0:T(8,128)(2,1)} %param.10) | copy-start | bytes 1179652
  7.2 11.2 %copy-start.5 = (s32[1,128]{1,0:T(1,128)S(1)}, s32[1,128]{1,0:T(1,128)}, u32[]{:S(2)}) copy-start(s32[1,128]{1,0:T(1,128)} %param.11) | copy-start | bytes 1540
  7.2 5.4 %copy-start.3 = (bf16[1,128,256]{2,1,0:T(8,128)(2,1)S(1)}, bf16[1,128,256]{2,1,0:T(8,128)(2,1)}, u32[]{:S(2)}) copy-start(bf16[1,128,256]{2,1,0:T(8,128)(2,1)} %param.13) | copy-start | bytes 196612
  7.2 52.6 %all-gather.3.cloned.1.call-start = ((), (), s32[]{:S(2)}) async-start(), calls=%async_computation.1 | async-start | bytes 1824768 | tf_op jit(solution)/shard_map/all_gather | solution.py:56
  10.4 51.9 %copy-start.4 = (s32[1,128]{1,0:T(1,128)S(1)}, s32[1,128]{1,0:T(1,128)}, u32[]{:S(2)}) copy-start(s32[1,128]{1,0:T(1,128)} %param.12) | copy-start | bytes 1540
  12.5 107.5 %all-reduce.3.cloned.1.call-start = ((), (), s32[]{:S(2)}) async-start(), calls=%async_computation | async-start | bytes 1179648 | tf_op jit(solution)/shard_map/psum | solution.py:121
  59.8 3.0 %copy-start.1 = (bf16[384,384]{1,0:T(8,128)(2,1)S(1)}, bf16[384,384]{1,0:T(8,128)(2,1)}, u32[]{:S(2)}) copy-start(bf16[384,384]{1,0:T(8,128)(2,1)} %param.15) | copy-start | bytes 884740
  62.8 1.1 copy-start.2
Sparse Core Ops, SparseCore 0:
  12.6 47.1 all-gather.2
  66.2 53.7 all-reduce.2
where the time goes:
time: 130 us
  waiting for transfers between devices  93.8 us (72%)
  between operations  14.2 us (11%)
  matrix products  7.21 us (6%)
  other arithmetic  5.94 us (5%)
  blocking collectives  5.86 us (5%)
  local copies, waits for them, and re-layouts  2.75 us (2%)
    psum x1, waiting for transfers between devices, shards(): lax.psum(jnp.stack([local_dw, local_aw]).astype(jnp.bfloat16), ('dp', 'se...  52.4 us
    all_gather x1, waiting for transfers between devices, shards(): gathered = lax.all_gather(packed, ('seq', 'head'), axis=1, tiled=False)  41.4 us
    all_gather x1, blocking collectives, shards(): target_all = lax.all_gather(target, 'seq', axis=1, tiled=True)  5.86 us
  transfers between devices with their start and end apart: 2, of which 2 were waited for; matrix products, arithmetic and copies ran while one was open for 1% of the time, Pallas kernels for 0%

commit v1 on v0

--- a/solution.py
+++ b/solution.py
@@ -118,7 +118,11 @@
     local_aw = jnp.einsum(
         "bnc,bnp->cp", acceptor_rows, acceptor_grad, preferred_element_type=jnp.float32
     )
-    summed = lax.psum(jnp.stack([local_dw, local_aw]).astype(jnp.bfloat16), ("dp", "seq"))
+
+    def things_lead(x_in, across):
+        return jnp.sum(lax.all_gather(x_in, across), axis=0)
+
+    summed = things_lead(jnp.stack([local_dw, local_aw]).astype(jnp.bfloat16), ("dp", "seq"))
     part = width // n_seq
     mine = lax.dynamic_slice_in_dim(summed, slab * part, part, 2).astype(jnp.float32)
     return (row_grad.astype(jnp.bfloat16), mine[0], mine[1])

time: 130 us -> 115 us (0.88)
  waiting for transfers between devices: 93.8 us -> 76.5 us
  other arithmetic: 5.94 us -> 8.05 us
    psum x1 -> x0, waiting for transfers between devices: 52.4 us -> none  [shards(): lax.psum(jnp.stack([local_dw, local_aw]).astype(jnp.bfloat16), ('dp', 'se...]
    all_gather x0 -> x1, waiting for transfers between devices: none -> 35.1 us  [things_lead(): return jnp.sum(lax.all_gather(x_in, across), axis=0)]
    reduce_sum x0 -> x1, other arithmetic: none -> 3.18 us  [things_lead(): return jnp.sum(lax.all_gather(x_in, across), axis=0)]
  transfers between devices with their start and end apart: 2 -> 2, of which waited for: 2 -> 2; matrix products, arithmetic and copies ran while one was open for 1% -> 2% of each run, Pallas kernels for 0% -> 0%
where the time goes in v1:
time: 115 us
  waiting for transfers between devices  76.5 us (67%)
  between operations  14.3 us (12%)
  other arithmetic  8.05 us (7%)
  matrix products  7.21 us (6%)
  blocking collectives  5.86 us (5%)
  local copies, waits for them, and re-layouts  2.75 us (2%)
    all_gather x1, waiting for transfers between devices, shards(): gathered = lax.all_gather(packed, ('seq', 'head'), axis=1, tiled=False)  41.4 us
    all_gather x1, waiting for transfers between devices, things_lead(): return jnp.sum(lax.all_gather(x_in, across), axis=0)  35.1 us
    all_gather x1, blocking collectives, shards(): target_all = lax.all_gather(target, 'seq', axis=1, tiled=True)  5.86 us
    reduce_sum x1, other arithmetic, things_lead(): return jnp.sum(lax.all_gather(x_in, across), axis=0)  3.18 us
    another operation x2, other arithmetic  2.39 us
  transfers between devices with their start and end apart: 2, of which 2 were waited for; matrix products, arithmetic and copies ran while one was open for 2% of the time, Pallas kernels for 0%

profile of v1, /device:TPU:0, one launch (start us, length us, event | category | flops | bytes accessed | tf_op | source)
XLA Modules:
  0.0 114.7 jit_solution(15813703713643450030)
XLA Ops:
  7.2 0.0 copy-start
  7.2 0.0 copy-start.5
  7.2 0.0 copy-start.3
  7.2 0.0 all-gather.6.cloned.1.call-start
  7.3 0.7 compare_bitcast_fusion
  8.0 0.7 subtract_bitcast_fusion
  8.7 0.0 copy-done
  8.7 0.3 convolution_convert_fusion.5
  8.9 0.3 convolution_convert_fusion.3
  9.2 1.2 %fusion.7 = bf16[1,128,384]{2,1,0:T(8,128)(2,1)S(1)} fusion(bf16[128,384]{1,0:T(8,128)(2,1)S(1)} %convolution_convert_fusion.5, bf16[384,384]{1,0:T(8,128)(2,1)} %param.14), kind=kOutput, calls=%fused_computation.19 | convolution fusion | flops 37797888 | bytes 491520 | tf_op jit(solution)/shard_map/bnc,cp->bnp/dot_general | solution.py:45
  10.4 0.0 copy-start.4
  10.4 1.2 %fusion.8 = bf16[1,128,384]{2,1,0:T(8,128)(2,1)S(1)} fusion(bf16[128,384]{1,0:T(8,128)(2,1)S(1)} %convolution_convert_fusion.3, bf16[384,384]{1,0:T(8,128)(2,1)} %param.15), kind=kOutput, calls=%fused_computation.20 | convolution fusion | flops 37797888 | bytes 491520 | tf_op jit(solution)/shard_map/bnc,cp->bnp/dot_general | solution.py:48
  11.6 0.2 scatter.14
  11.8 0.7 pad_maximum_fusion.1
  12.5 0.0 all-gather.6.cloned.1.call-update
  12.5 0.0 all-gather.4.cloned.1.call-start
  12.5 0.0 copy-done.3
  12.6 5.9 %all_gather.15 = bf16[1,256,256]{2,1,0:T(8,128)(2,1)S(1)} all-gather(bf16[1,128,256]{2,1,0:T(8,128)(2,1)S(1)} %copy-done.3), channel_id=1, replica_groups=mesh['dp'=4,'seq'=2,'head'=4] {'seq'}, dimensions={1}, use_global_device_ids=true | all-gather | bytes 196608 | tf_op jit(solution)/shard_map/all_gather | solution.py:36
  18.4 0.0 copy-done.5
  18.4 41.4 %all-gather.6.cloned.1.call-done = bf16[8,264,384]{2,1,0:T(8,128)(2,1)} async-done(((bf16[1,264,384]{2,1,0:T(8,128)(2,1)}), bf16[8,264,384]{2,1,0:T(8,128)(2,1)}) %all-gather.6.cloned.1.call-update) | async-done | bytes 1622032 | tf_op jit(solution)/shard_map/all_gather | solution.py:56
  59.8 0.8 fusion.91
  60.6 1.7 %add_convert_fusion.1 = (bf16[1,2,1,128,384]{4,3,2,1,0:T(8,128)(2,1)S(1)}, bf16[1,2,1,128,384]{4,3,2,1,0:T(8,128)(2,1)S(1)}) fusion(bf16[1,2,4,264,384]{4,3,2,1,0:T(8,128)(2,1)} %bitcast.140), kind=kLoop, calls=%fused_computation.28 | loop fusion | flops 1572864 | bytes 1966080 | tf_op jit(solution)/shard_map/convert.10
  62.2 0.0 copy-done.4
  62.3 0.6 fusion.6
  62.8 0.3 fusion.4
  63.1 0.5 fusion.5
  63.6 0.0 copy-start.1
  63.6 0.0 copy-start.2
  63.7 0.3 fusion.3
  63.9 0.9 pad_maximum_fusion
  64.8 0.0 all-gather.4.cloned.1.call-update
  64.8 0.0 copy-done.1
  64.8 0.2 fusion.93
  65.1 0.0 copy-done.2
  65.1 0.2 fusion.92
  65.3 0.4 fusion.11
  65.7 0.4 fusion.12
  66.1 0.4 convolution_add_fusion.1
  66.5 1.1 fusion.2
  67.6 35.1 %all-gather.4.cloned.1.call-done = bf16[8,2,384,384]{3,2,1,0:T(8,128)(2,1)} async-done(((bf16[1,2,384,384]{3,2,1,0:T(8,128)(2,1)}), bf16[8,2,384,384]{3,2,1,0:T(8,128)(2,1)}) %all-gather.4.cloned.1.call-update) | async-done | bytes 4718608 | tf_op jit(solution)/shard_map/all_gather | solution.py:123
  102.7 3.2 %reduce_sum.12 = bf16[2,384,384]{2,1,0:T(8,128)(2,1)S(1)} reduce(bf16[8,2,384,384]{3,2,1,0:T(8,128)(2,1)} %all-gather.4.cloned.1.call-done, bf16[]{:T(256)} %constant.115.clone.1), dimensions={0}, to_apply=%region_0.0 | reduce | flops 2064384 | bytes 5308418 | tf_op jit(solution)/shard_map/reduce_sum | solution.py:123
  105.9 0.2 dynamic-slice_convert_fusion
  106.1 0.1 slice_bitcast_fusion
  106.2 0.9 copy.13
  107.0 0.9 copy.14
  (4 shorter events, 0.0 us)
Async XLA Ops:
  7.2 1.5 %copy-start = (bf16[1,512,384]{2,1,0:T(8,128)(2,1)S(1)}, bf16[1,512,384]{2,1,0:T(8,128)(2,1)}, u32[]{:S(2)}) copy-start(bf16[1,512,384]{2,1,0:T(8,128)(2,1)} %param.10) | copy-start | bytes 1179652
  7.2 11.2 %copy-start.5 = (s32[1,128]{1,0:T(1,128)S(1)}, s32[1,128]{1,0:T(1,128)}, u32[]{:S(2)}) copy-start(s32[1,128]{1,0:T(1,128)} %param.11) | copy-start | bytes 1540
  7.2 5.4 %copy-start.3 = (bf16[1,128,256]{2,1,0:T(8,128)(2,1)S(1)}, bf16[1,128,256]{2,1,0:T(8,128)(2,1)}, u32[]{:S(2)}) copy-start(bf16[1,128,256]{2,1,0:T(8,128)(2,1)} %param.13) | copy-start | bytes 196612
  7.2 52.6 %all-gather.6.cloned.1.call-start = ((), (), s32[]{:S(2)}) async-start(), calls=%async_computation.1 | async-start | bytes 1824768 | tf_op jit(solution)/shard_map/all_gather | solution.py:56
  10.4 51.9 %copy-start.4 = (s32[1,128]{1,0:T(1,128)S(1)}, s32[1,128]{1,0:T(1,128)}, u32[]{:S(2)}) copy-start(s32[1,128]{1,0:T(1,128)} %param.12) | copy-start | bytes 1540
  12.5 90.2 %all-gather.4.cloned.1.call-start = ((), (), s32[]{:S(2)}) async-start(), calls=%async_computation | async-start | bytes 5308416 | tf_op jit(solution)/shard_map/all_gather | solution.py:123
  63.6 1.2 %copy-start.1 = (bf16[384,384]{1,0:T(8,128)(2,1)S(1)}, bf16[384,384]{1,0:T(8,128)(2,1)}, u32[]{:S(2)}) copy-start(bf16[384,384]{1,0:T(8,128)(2,1)} %param.15) | copy-start | bytes 884740
  63.6 1.4 %copy-start.2 = (bf16[384,384]{1,0:T(8,128)(2,1)S(1)}, bf16[384,384]{1,0:T(8,128)(2,1)}, u32[]{:S(2)}) copy-start(bf16[384,384]{1,0:T(8,128)(2,1)} %param.14) | copy-start | bytes 884740
Sparse Core Ops, SparseCore 0:
  12.6 47.1 all-gather.5
  65.0 37.7 all-gather.3
